TPU v7x, 256 devices: a whole 4x4x8 slice. The times are simulated.
256 devices in a mesh: grp: 8 (over x_hi, y), dev: 32 (over z, x_lo, core).
Axes of the slice: x: 4 (x_hi: 2, x_lo: 2; x = x_hi * 2 + x_lo), y: 4, z: 8, core: 2. Of those that a mesh axis runs over, the one named last changes fastest.
Arguments:
- slab: bfloat16 [16, 8000, 8000], P('grp', 'dev'), may hold values from -2.5 to 2.5
- orbitals: bfloat16 [8000, 640], P('dev'), may hold values from -0.0625 to 0.0625
- hcore: float32 [8000, 8000], P('dev', 'grp'), may hold values from -6 to 6
- metric_inv: float32 [16, 16], replicated, may hold values from -1 to 2, as said below
Outputs:
- fock: float32 [8000, 8000], P('dev', 'grp')
Inputs may be any that keep to these rules, and one draw needn't show every extreme that they name: `metric_inv`: symmetric.
All inputs are finite; a program needn't handle non-finite values.
Results may differ from a plain program's by a relative error of at most 0.0065.
Values may be sent and summed in bfloat16 or wider, within the bound.
No kernel may reach another device: no remote copies, remote signals or barrier semaphores. Data moves between devices by JAX's collectives and lax.ppermute only.
A program may use at most 192 MiB of HBM per device.

v0:
```python
import jax
import jax.numpy as jnp
from jax import lax
from jax.sharding import PartitionSpec as P


def shards(slab, orbitals, hcore, metric_inv):
    aux_count = slab.shape[0]
    row_count = slab.shape[1]
    full_width = slab.shape[2]
    occ_count = orbitals.shape[1]
    slab_flat = slab.reshape(aux_count * row_count, full_width)
    half_done = jnp.dot(
        slab_flat,
        lax.all_gather(orbitals, "dev", axis=0, tiled=True),
        preferred_element_type=jnp.float32,
    )
    half_done = half_done.astype(jnp.bfloat16).reshape(aux_count, row_count, occ_count)
    aux_density = jnp.sum(
        half_done.astype(jnp.float32) * orbitals.astype(jnp.float32)[None], axis=(1, 2)
    )
    group_index = lax.axis_index("grp")
    group_density = lax.psum(aux_density, "dev")
    density_all = lax.all_gather(group_density, "grp", axis=0, tiled=True)
    fit_coef = jnp.dot(metric_inv, density_all, precision=lax.Precision.HIGHEST)
    half_flat = jnp.transpose(half_done, (1, 0, 2)).reshape(row_count, aux_count * occ_count)
    exchange_part = lax.dot_general(
        half_flat,
        lax.all_gather(half_flat, "dev", axis=0, tiled=True),
        (((1,), (1,)), ((), ())),
        preferred_element_type=jnp.float32,
    )
    local_coef = lax.dynamic_slice_in_dim(fit_coef, group_index * aux_count, aux_count)
    coulomb_part = jnp.zeros((row_count, full_width), jnp.float32)
    for aux_index in range(aux_count):
        coulomb_part = coulomb_part + local_coef[aux_index] * slab[aux_index].astype(jnp.float32)
    reduced = lax.psum_scatter(
        2.0 * coulomb_part - exchange_part, "grp", scatter_dimension=1, tiled=True
    )
    fock = hcore + reduced
    return fock


def solution(mesh):
    return jax.shard_map(
        shards,
        mesh=mesh,
        in_specs=(P("grp", "dev", None), P("dev", None), P("dev", "grp"), P()),
        out_specs=P("dev", "grp"),
        check_vma=False,
    )
```

profile of v0, /device:TPU:2, one launch (start us, length us, event | category | flops | bytes accessed | tf_op | source)
XLA Modules:
  0.0 402.7 jit_solution(6335460769524792547)
XLA Ops:
  6.5 0.0 copy-start
  6.5 0.0 all-gather.5.cloned.1.call-start
  6.5 0.7 all-gather.5.cloned.1.call-update
  7.3 0.0 all-gather.7.cloned.1.call-start
  7.3 1.1 mul.37
  8.4 0.1 mul.38
  8.5 7.4 %copy.19 = bf16[2,250,8000]{2,1,0:T(8,128)(2,1)} copy(bf16[2,250,8000]{2,0,1:T(2,128)(2,1)} %param.4) | data formatting | bytes 16000000 | tf_op args[0]
  15.9 10.1 %reshape.21 = bf16[500,8000]{1,0:T(8,128)(2,1)} reshape(bf16[2,250,8000]{2,1,0:T(8,128)(2,1)} %copy.19) | data formatting | bytes 16000000 | tf_op jit(solution)/shard_map/reshape | solution.py:12
  25.9 60.3 %all-gather.5.cloned.1.call-done = bf16[32,250,640]{2,1,0:T(8,128)(2,1)} async-done(((bf16[1,250,640]{2,1,0:T(8,128)(2,1)}), bf16[32,250,640]{2,1,0:T(8,128)(2,1)}) %all-gather.5.cloned.1.call-update) | async-done | bytes 10240016 | tf_op jit(solution)/shard_map/all_gather | solution.py:15
  86.2 10.9 %reshape.28 = bf16[8000,640]{1,0:T(8,128)(2,1)} reshape(bf16[32,250,640]{2,1,0:T(8,128)(2,1)} %all-gather.5.cloned.1.call-done) | data formatting | bytes 20480000
  97.2 12.2 %multiply_reduce_fusion = (f32[500]{0:T(512)S(1)}, bf16[500,640]{1,0:T(8,128)(2,1)S(1)}) fusion(f32[500,640]{1,0:T(8,128)S(1)} %mul.38, bf16[500,8000]{1,0:T(8,128)(2,1)} %reshape.21, bf16[8000,640]{1,0:T(8,128)(2,1)} %reshape.28), kind=kOutput, calls=%fused_computation.2 | convolution fusion | flops 5121279488 | bytes 20162000 | tf_op jit(solution)/shard_map/dot_general | solution.py:13
  109.4 0.1 reshape.22
  109.5 0.3 copy.22
  109.8 1.1 copy.24
  110.9 0.0 all-gather.7.cloned.1.call-update
  110.9 0.0 reduce-scatter.2.cloned.1.call-start
  111.0 17.1 %fusion.1 = (bf16[1,250,8000]{2,0,1:T(2,128)(2,1)}, bf16[1,250,8000]{2,0,1:T(2,128)(2,1)}) fusion(bf16[2,250,8000]{2,0,1:T(2,128)(2,1)} %param.4), kind=kLoop, calls=%fused_computation.5 | loop fusion | bytes 16000000 | tf_op jit(solution)/shard_map/slice | solution.py:36
  128.1 17.3 %copy.25 = bf16[1,250,8000]{1,2,0:T(8,128)(2,1)} copy(bf16[1,250,8000]{2,0,1:T(2,128)(2,1)} %get-tuple-element.5) | data formatting | bytes 8000000
  145.4 0.0 copy-start.2
  145.4 17.3 %copy.26 = bf16[1,250,8000]{1,2,0:T(8,128)(2,1)} copy(bf16[1,250,8000]{2,0,1:T(2,128)(2,1)} %get-tuple-element.6) | data formatting | bytes 8000000
  162.7 0.0 copy-done.2
  162.7 0.6 dynamic-slice.1
  163.3 0.1 reduce_sum.14
  163.4 0.1 reduce_sum.18
  164.1 52.8 %psum.7 = f32[2]{0:T(128)S(1)} all-reduce(f32[2]{0:T(128)S(1)} %reduce_sum.18), channel_id=1, replica_groups=mesh['grp'=8,'dev'=32] {'dev'}, use_global_device_ids=true, to_apply=%region_2.0 | all-reduce | flops 2 | bytes 16 | tf_op jit(solution)/shard_map/psum | solution.py:23
  216.9 0.2 dynamic-update-slice
  217.2 24.1 %all-reduce = f32[16]{0:T(128)S(1)} all-reduce(f32[16]{0:T(128)S(1)} %dynamic-update-slice), channel_id=1, replica_groups=mesh['grp'=8,'dev'=32] {'grp'}, use_global_device_ids=true, to_apply=%add | all-reduce | flops 16 | bytes 128
  241.3 0.0 copy-done
  241.3 0.1 convolution_bitcast_fusion
  241.4 0.1 dynamic_slice.3
  241.5 0.6 fusion.2
  242.1 0.0 all-gather.7.cloned.1.call-done
  242.1 17.5 %reshape.30 = bf16[8000,1280]{1,0:T(8,128)(2,1)} reshape(bf16[32,250,1280]{2,1,0:T(8,128)(2,1)} %all-gather.7.cloned.1.call-done) | data formatting | bytes 40960000
  259.6 15.5 %convolution_subtract_fusion = f32[250,8000]{0,1:T(8,128)} fusion(bf16[250,1280]{0,1:T(8,128)(2,1)S(1)} %bitcast.20, bf16[8000,1280]{1,0:T(8,128)(2,1)} %reshape.30, bf16[1,250,8000]{1,2,0:T(8,128)(2,1)} %copy.26, bf16[1,250,8000]{1,2,0:T(8,128)(2,1)} %copy.25, f32[]{:T(128)} %bitcast.5, f32[]{:T(128)} %bitcast.4), kind=kOutput, calls=%fused_computation | convolution fusion | flops 5134000128 | bytes 37120008 | tf_op jit(solution)/shard_map/dot_general | solution.py:27
  275.1 0.0 copy-start.1
  275.1 0.0 reduce-scatter.2.cloned.1.call-update
  275.1 118.6 %reduce-scatter.2.cloned.1.call-done = f32[250,1000]{0,1:T(8,128)} async-done(((f32[250,8000]{0,1:T(8,128)}), f32[250,1000]{0,1:T(8,128)}) %reduce-scatter.2.cloned.1.call-update) | async-done | bytes 1000016 | tf_op jit(solution)/shard_map/reduce_scatter | solution.py:37
  393.8 0.0 copy-done.1
  393.8 2.4 add.16
  (1 shorter events, 0.0 us)
Async XLA Ops:
  6.5 234.7 %copy-start = (f32[16,16]{1,0:T(8,128)S(1)}, f32[16,16]{1,0:T(8,128)}, u32[]{:S(2)}) copy-start(f32[16,16]{1,0:T(8,128)} %param.7) | copy-start | bytes 3076
  6.5 79.7 %all-gather.5.cloned.1.call-start = ((), (), s32[]{:S(2)}) async-start(), calls=%async_computation.2 | async-start | bytes 10813440 | tf_op jit(solution)/shard_map/all_gather | solution.py:15
  7.3 234.8 %all-gather.7.cloned.1.call-start = ((), (), s32[]{:S(2)}) async-start(), calls=%async_computation.3 | async-start | bytes 21626880 | tf_op jit(solution)/shard_map/all_gather | solution.py:29
  110.9 282.9 %reduce-scatter.2.cloned.1.call-start = ((), (), s32[]{:S(2)}) async-start(), calls=%async_computation.1 | async-start | bytes 9216000 | tf_op jit(solution)/shard_map/reduce_scatter | solution.py:37
  145.4 17.3 %copy-start.2 = (u32[256]{0:T(256)S(1)}, u32[256]{0:T(256)}, u32[]{:S(2)}) copy-start(u32[256]{0:T(256)} %constant.21) | copy-start | bytes 3076
  275.1 118.7 %copy-start.1 = (f32[250,1000]{0,1:T(8,128)S(1)}, f32[250,1000]{0,1:T(8,128)}, u32[]{:S(2)}) copy-start(f32[250,1000]{0,1:T(8,128)} %param.6) | copy-start | bytes 3000004
Sparse Core Ops, SparseCore 0:
  9.2 77.0 all-gather.4
  111.0 120.4 all-gather.6
  275.3 118.4 reduce-scatter.1
where the time goes:
time: 405 us; the launch traced here: 403 us
  waiting for transfers between devices  180 us (44%)
  local copies, waits for them, and re-layouts  102 us (25%)
  blocking collectives  76.9 us (19%)
  matrix products  27.8 us (7%)
  between operations  13.8 us (3%)
    reduce_scatter x1, waiting for transfers between devices, shards(): lax.psum_scatter(2.0 * coulomb_part - exchange_part, 'grp', scatter_dimen...  119 us
    unnamed x15, local copies, waits for them, and re-layouts  72.3 us
    all_gather x1, waiting for transfers between devices, shards(): lax.all_gather(orbitals, 'dev', axis=0, tiled=True)  60.3 us
    psum x1, blocking collectives, shards(): group_density = lax.psum(aux_density, 'dev')  52.8 us
    unnamed x1, blocking collectives  24.1 us
    slice x1, local copies, waits for them, and re-layouts, shards(): slab[aux_index].astype(jnp.float32)  17.1 us
    dot_general x1, matrix products, shards(): lax.dot_general(half_flat, lax.all_gather(half_flat, 'dev', axis=0, tiled...  15.5 us
    dot_general x1, matrix products, shards(): jnp.dot(slab_flat, lax.all_gather(orbitals, 'dev', axis=0, tiled=True), p...  12.2 us
  transfers between devices with their start and end apart: 3, of which 2 were waited for; matrix products, arithmetic and copies ran while one was open for 18% of the time, Pallas kernels for 0%

commit v1 on v0

--- a/solution.py
+++ b/solution.py
@@ -34,9 +34,11 @@
     coulomb_part = jnp.zeros((row_count, full_width), jnp.float32)
     for aux_index in range(aux_count):
         coulomb_part = coulomb_part + local_coef[aux_index] * slab[aux_index].astype(jnp.float32)
-    reduced = lax.psum_scatter(
-        2.0 * coulomb_part - exchange_part, "grp", scatter_dimension=1, tiled=True
-    )
+    group_count = lax.psum(1, "grp")
+    partial = (2.0 * coulomb_part - exchange_part).astype(jnp.bfloat16)
+    partial = partial.reshape(row_count, group_count, full_width // group_count)
+    pieces = lax.all_to_all(partial, "grp", 1, 1, tiled=True)
+    reduced = jnp.sum(pieces.astype(jnp.float32), axis=1)
     fock = hcore + reduced
     return fock
 

time: 405 us -> 336 us (0.83)
  waiting for transfers between devices: 180 us -> 61 us
  blocking collectives: 76.9 us -> 125 us
    reduce_scatter x1 -> x0, waiting for transfers between devices: 119 us -> none  [shards(): lax.psum_scatter(2.0 * coulomb_part - exchange_part, 'grp', scatter_dimen...]
    all_to_all x0 -> x1, blocking collectives: none -> 48.6 us  [shards(): pieces = lax.all_to_all(partial, 'grp', 1, 1, tiled=True)]
  transfers between devices with their start and end apart: 3 -> 2, of which waited for: 2 -> 1; matrix products, arithmetic and copies ran while one was open for 18% -> 22% of each run, Pallas kernels for 0% -> 0%
where the time goes in v1:
time: 336 us; the launch traced here: 332 us
  blocking collectives  125 us (37%)
  local copies, waits for them, and re-layouts  102 us (30%)
  waiting for transfers between devices  61 us (18%)
  matrix products  27.4 us (8%)
  between operations  14.1 us (4%)
    unnamed x15, local copies, waits for them, and re-layouts  72.4 us
    all_gather x1, waiting for transfers between devices, shards(): lax.all_gather(orbitals, 'dev', axis=0, tiled=True)  60.3 us
    psum x1, blocking collectives, shards(): group_density = lax.psum(aux_density, 'dev')  52.8 us
    all_to_all x1, blocking collectives, shards(): pieces = lax.all_to_all(partial, 'grp', 1, 1, tiled=True)  48.6 us
    unnamed x1, blocking collectives  24.1 us
    slice x1, local copies, waits for them, and re-layouts, shards(): slab[aux_index].astype(jnp.float32)  17.2 us
    dot_general x1, matrix products, shards(): lax.dot_general(half_flat, lax.all_gather(half_flat, 'dev', axis=0, tiled...  15 us
    dot_general x1, matrix products, shards(): jnp.dot(slab_flat, lax.all_gather(orbitals, 'dev', axis=0, tiled=True), p...  12.2 us
  transfers between devices with their start and end apart: 2, of which 1 were waited for; matrix products, arithmetic and copies ran while one was open for 22% of the time, Pallas kernels for 0%

profile of v1, /device:TPU:2, one launch (start us, length us, event | category | flops | bytes accessed | tf_op | source)
XLA Modules:
  0.0 332.0 jit_solution(7535997628521245111)
XLA Ops:
  6.5 0.0 copy-start
  6.5 0.0 all-gather.5.cloned.1.call-start
  6.5 0.7 all-gather.5.cloned.1.call-update
  7.3 0.0 all-gather.7.cloned.1.call-start
  7.3 1.1 mul.37
  8.4 0.1 mul.38
  8.5 7.4 %copy.19 = bf16[2,250,8000]{2,1,0:T(8,128)(2,1)} copy(bf16[2,250,8000]{2,0,1:T(2,128)(2,1)} %param.4) | data formatting | bytes 16000000 | tf_op args[0]
  15.9 10.1 %reshape.24 = bf16[500,8000]{1,0:T(8,128)(2,1)} reshape(bf16[2,250,8000]{2,1,0:T(8,128)(2,1)} %copy.19) | data formatting | bytes 16000000 | tf_op jit(solution)/shard_map/reshape | solution.py:12
  25.9 60.3 %all-gather.5.cloned.1.call-done = bf16[32,250,640]{2,1,0:T(8,128)(2,1)} async-done(((bf16[1,250,640]{2,1,0:T(8,128)(2,1)}), bf16[32,250,640]{2,1,0:T(8,128)(2,1)}) %all-gather.5.cloned.1.call-update) | async-done | bytes 10240016 | tf_op jit(solution)/shard_map/all_gather | solution.py:15
  86.3 10.9 %reshape.32 = bf16[8000,640]{1,0:T(8,128)(2,1)} reshape(bf16[32,250,640]{2,1,0:T(8,128)(2,1)} %all-gather.5.cloned.1.call-done) | data formatting | bytes 20480000
  97.2 12.2 %multiply_reduce_fusion = (f32[500]{0:T(512)S(1)}, bf16[500,640]{1,0:T(8,128)(2,1)S(1)}) fusion(f32[500,640]{1,0:T(8,128)S(1)} %mul.38, bf16[500,8000]{1,0:T(8,128)(2,1)} %reshape.24, bf16[8000,640]{1,0:T(8,128)(2,1)} %reshape.32), kind=kOutput, calls=%fused_computation.4 | convolution fusion | flops 5121279488 | bytes 20162000 | tf_op jit(solution)/shard_map/dot_general | solution.py:13
  109.4 0.1 reshape.25
  109.5 0.3 copy.22
  109.8 1.1 copy.24
  110.9 0.0 all-gather.7.cloned.1.call-update
  110.9 17.2 %fusion.2 = (bf16[1,250,8000]{2,0,1:T(2,128)(2,1)}, bf16[1,250,8000]{2,0,1:T(2,128)(2,1)}) fusion(bf16[2,250,8000]{2,0,1:T(2,128)(2,1)} %param.4), kind=kLoop, calls=%fused_computation.7 | loop fusion | bytes 16000000 | tf_op jit(solution)/shard_map/slice | solution.py:36
  128.1 17.3 %copy.25 = bf16[1,250,8000]{1,2,0:T(8,128)(2,1)} copy(bf16[1,250,8000]{2,0,1:T(2,128)(2,1)} %get-tuple-element.5) | data formatting | bytes 8000000
  145.4 0.0 copy-start.2
  145.4 17.3 %copy.26 = bf16[1,250,8000]{1,2,0:T(8,128)(2,1)} copy(bf16[1,250,8000]{2,0,1:T(2,128)(2,1)} %get-tuple-element.6) | data formatting | bytes 8000000
  162.7 0.0 copy-done.2
  162.7 0.6 dynamic-slice.1
  163.3 0.1 reduce_sum.26
  163.4 0.1 reduce_sum.27
  164.2 52.8 %psum.7 = f32[2]{0:T(128)S(1)} all-reduce(f32[2]{0:T(128)S(1)} %reduce_sum.27), channel_id=1, replica_groups=mesh['grp'=8,'dev'=32] {'dev'}, use_global_device_ids=true, to_apply=%region_2.0 | all-reduce | flops 2 | bytes 16 | tf_op jit(solution)/shard_map/psum | solution.py:23
  217.0 0.2 dynamic-update-slice
  217.2 24.1 %all-reduce = f32[16]{0:T(128)S(1)} all-reduce(f32[16]{0:T(128)S(1)} %dynamic-update-slice), channel_id=1, replica_groups=mesh['grp'=8,'dev'=32] {'grp'}, use_global_device_ids=true, to_apply=%add | all-reduce | flops 16 | bytes 128
  241.3 0.0 copy-done
  241.3 0.1 convolution_bitcast_fusion
  241.4 0.1 dynamic_slice.3
  241.5 0.6 fusion.3
  242.1 0.0 all-gather.7.cloned.1.call-done
  242.1 17.5 %reshape.34 = bf16[8000,1280]{1,0:T(8,128)(2,1)} reshape(bf16[32,250,1280]{2,1,0:T(8,128)(2,1)} %all-gather.7.cloned.1.call-done) | data formatting | bytes 40960000
  259.6 15.0 %fusion = bf16[250,8000]{0,1:T(8,128)(2,1)} fusion(bf16[250,1280]{0,1:T(8,128)(2,1)S(1)} %bitcast.22, bf16[8000,1280]{1,0:T(8,128)(2,1)} %reshape.34, bf16[1,250,8000]{1,2,0:T(8,128)(2,1)} %copy.26, bf16[1,250,8000]{1,2,0:T(8,128)(2,1)} %copy.25, f32[]{:T(128)} %bitcast.5, f32[]{:T(128)} %bitcast.4), kind=kOutput, calls=%fused_computation.1 | convolution fusion | flops 5136000000 | bytes 33120008 | tf_op jit(solution)/shard_map/dot_general | solution.py:27
  274.7 0.0 copy-start.1
  274.7 48.6 %all_to_all.5 = bf16[250,8,1000]{0,2,1:T(8,128)(2,1)S(1)} all-to-all(bf16[250,8,1000]{0,2,1:T(8,128)(2,1)} %bitcast.20), channel_id=1, replica_groups=mesh['grp'=8,'dev'=32] {'grp'}, dimensions={1} | all-to-all | bytes 8000000 | tf_op jit(solution)/shard_map/all_to_all | solution.py:40
  323.2 0.7 convert_reduce_fusion
  324.0 0.0 copy-done.1
  324.0 1.2 add.14
  (1 shorter events, 0.0 us)
Async XLA Ops:
  6.5 234.8 %copy-start = (f32[16,16]{1,0:T(8,128)S(1)}, f32[16,16]{1,0:T(8,128)}, u32[]{:S(2)}) copy-start(f32[16,16]{1,0:T(8,128)} %param.7) | copy-start | bytes 3076
  6.5 79.7 %all-gather.5.cloned.1.call-start = ((), (), s32[]{:S(2)}) async-start(), calls=%async_computation.1 | async-start | bytes 10813440 | tf_op jit(solution)/shard_map/all_gather | solution.py:15
  7.3 234.9 %all-gather.7.cloned.1.call-start = ((), (), s32[]{:S(2)}) async-start(), calls=%async_computation.2 | async-start | bytes 21626880 | tf_op jit(solution)/shard_map/all_gather | solution.py:29
  145.4 17.3 %copy-start.2 = (u32[256]{0:T(256)S(1)}, u32[256]{0:T(256)}, u32[]{:S(2)}) copy-start(u32[256]{0:T(256)} %constant.21) | copy-start | bytes 3076
  274.7 49.3 %copy-start.1 = (f32[250,1000]{0,1:T(8,128)S(1)}, f32[250,1000]{0,1:T(8,128)}, u32[]{:S(2)}) copy-start(f32[250,1000]{0,1:T(8,128)} %param.6) | copy-start | bytes 3000004
Sparse Core Ops, SparseCore 0:
  9.2 77.0 all-gather.4
  111.0 120.4 all-gather.6

commit v2 on v1

--- a/solution.py
+++ b/solution.py
@@ -20,8 +20,10 @@
         half_done.astype(jnp.float32) * orbitals.astype(jnp.float32)[None], axis=(1, 2)
     )
     group_index = lax.axis_index("grp")
-    group_density = lax.psum(aux_density, "dev")
-    density_all = lax.all_gather(group_density, "grp", axis=0, tiled=True)
+    group_count = lax.psum(1, "grp")
+    density_slots = jnp.zeros((group_count, aux_count), jnp.float32)
+    density_slots = lax.dynamic_update_index_in_dim(density_slots, aux_density, group_index, 0)
+    density_all = lax.psum(density_slots, ("grp", "dev")).reshape(group_count * aux_count)
     fit_coef = jnp.dot(metric_inv, density_all, precision=lax.Precision.HIGHEST)
     half_flat = jnp.transpose(half_done, (1, 0, 2)).reshape(row_count, aux_count * occ_count)
     exchange_part = lax.dot_general(
@@ -34,7 +36,6 @@
     coulomb_part = jnp.zeros((row_count, full_width), jnp.float32)
     for aux_index in range(aux_count):
         coulomb_part = coulomb_part + local_coef[aux_index] * slab[aux_index].astype(jnp.float32)
-    group_count = lax.psum(1, "grp")
     partial = (2.0 * coulomb_part - exchange_part).astype(jnp.bfloat16)
     partial = partial.reshape(row_count, group_count, full_width // group_count)
     pieces = lax.all_to_all(partial, "grp", 1, 1, tiled=True)

time: 336 us -> 339 us (level)
  blocking collectives: 125 us -> 132 us
    psum x1, blocking collectives: 52.8 us -> 77.3 us  [shards(): lax.psum(density_slots, ('grp', 'dev')).reshape(group_count * aux_count)]
    unnamed x1 -> x0, blocking collectives: 24.1 us -> none
    all_to_all x1, blocking collectives: 48.6 us -> 54.6 us  [shards(): pieces = lax.all_to_all(partial, 'grp', 1, 1, tiled=True)]
    unnamed x15 -> x10, local copies, waits for them, and re-layouts: 72.4 us -> 71.5 us
  transfers between devices with their start and end apart: 2 -> 2, of which waited for: 1 -> 1; matrix products, arithmetic and copies ran while one was open for 22% -> 21% of each run, Pallas kernels for 0% -> 0%
where the time goes in v2:
time: 339 us; the launch traced here: 337 us
  blocking collectives  132 us (39%)
  local copies, waits for them, and re-layouts  101 us (30%)
  waiting for transfers between devices  61 us (18%)
  matrix products  27.4 us (8%)
  between operations  13.5 us (4%)
    psum x1, blocking collectives, shards(): lax.psum(density_slots, ('grp', 'dev')).reshape(group_count * aux_count)  77.3 us
    unnamed x10, local copies, waits for them, and re-layouts  71.5 us
    all_gather x1, waiting for transfers between devices, shards(): lax.all_gather(orbitals, 'dev', axis=0, tiled=True)  60.3 us
    all_to_all x1, blocking collectives, shards(): pieces = lax.all_to_all(partial, 'grp', 1, 1, tiled=True)  54.6 us
    slice x1, local copies, waits for them, and re-layouts, shards(): slab[aux_index].astype(jnp.float32)  17.2 us
    dot_general x1, matrix products, shards(): lax.dot_general(half_flat, lax.all_gather(half_flat, 'dev', axis=0, tiled...  15 us
    dot_general x1, matrix products, shards(): jnp.dot(slab_flat, lax.all_gather(orbitals, 'dev', axis=0, tiled=True), p...  12.2 us
    reshape x1, local copies, waits for them, and re-layouts, shards(): slab_flat = slab.reshape(aux_count * row_count, full_width)  10.1 us
  transfers between devices with their start and end apart: 2, of which 1 were waited for; matrix products, arithmetic and copies ran while one was open for 21% of the time, Pallas kernels for 0%

profile of v2, /device:TPU:2, one launch (start us, length us, event | category | flops | bytes accessed | tf_op | source)
XLA Modules:
  0.0 337.1 jit_solution(3047101780299509217)
XLA Ops:
  6.5 0.0 copy-start
  6.5 0.0 all-gather.5.cloned.1.call-start
  6.5 0.7 all-gather.5.cloned.1.call-update
  7.3 0.0 all-gather.7.cloned.1.call-start
  7.3 1.1 mul.37
  8.4 0.1 mul.38
  8.5 7.4 %copy.19 = bf16[2,250,8000]{2,1,0:T(8,128)(2,1)} copy(bf16[2,250,8000]{2,0,1:T(2,128)(2,1)} %param.4) | data formatting | bytes 16000000 | tf_op args[0]
  15.9 10.1 %reshape.27 = bf16[500,8000]{1,0:T(8,128)(2,1)} reshape(bf16[2,250,8000]{2,1,0:T(8,128)(2,1)} %copy.19) | data formatting | bytes 16000000 | tf_op jit(solution)/shard_map/reshape | solution.py:12
  25.9 60.3 %all-gather.5.cloned.1.call-done = bf16[32,250,640]{2,1,0:T(8,128)(2,1)} async-done(((bf16[1,250,640]{2,1,0:T(8,128)(2,1)}), bf16[32,250,640]{2,1,0:T(8,128)(2,1)}) %all-gather.5.cloned.1.call-update) | async-done | bytes 10240016 | tf_op jit(solution)/shard_map/all_gather | solution.py:15
  86.3 10.9 %reshape.33 = bf16[8000,640]{1,0:T(8,128)(2,1)} reshape(bf16[32,250,640]{2,1,0:T(8,128)(2,1)} %all-gather.5.cloned.1.call-done) | data formatting | bytes 20480000
  97.2 12.2 %multiply_reduce_fusion = (f32[500]{0:T(512)S(1)}, bf16[500,640]{1,0:T(8,128)(2,1)S(1)}) fusion(f32[500,640]{1,0:T(8,128)S(1)} %mul.38, bf16[500,8000]{1,0:T(8,128)(2,1)} %reshape.27, bf16[8000,640]{1,0:T(8,128)(2,1)} %reshape.33), kind=kOutput, calls=%fused_computation.4 | convolution fusion | flops 5121279488 | bytes 20162000 | tf_op jit(solution)/shard_map/dot_general | solution.py:13
  109.4 0.1 reshape.29
  109.5 0.3 copy.22
  109.8 1.1 copy.24
  110.9 0.0 all-gather.7.cloned.1.call-update
  110.9 17.2 %fusion.2 = (bf16[1,250,8000]{2,0,1:T(2,128)(2,1)}, bf16[1,250,8000]{2,0,1:T(2,128)(2,1)}) fusion(bf16[2,250,8000]{2,0,1:T(2,128)(2,1)} %param.4), kind=kLoop, calls=%fused_computation.7 | loop fusion | bytes 16000000 | tf_op jit(solution)/shard_map/slice | solution.py:38
  128.1 17.3 %copy.25 = bf16[1,250,8000]{1,2,0:T(8,128)(2,1)} copy(bf16[1,250,8000]{2,0,1:T(2,128)(2,1)} %get-tuple-element.5) | data formatting | bytes 8000000
  145.4 17.3 %copy.26 = bf16[1,250,8000]{1,2,0:T(8,128)(2,1)} copy(bf16[1,250,8000]{2,0,1:T(2,128)(2,1)} %get-tuple-element.6) | data formatting | bytes 8000000
  162.7 0.1 reduce_sum.26
  162.8 0.1 reduce_sum.27
  163.0 0.1 reshape.28
  163.0 77.3 %psum.7 = f32[16]{0:T(128)S(1)} all-reduce(f32[16]{0:T(128)S(1)} %reshape.28), channel_id=1, replica_groups=mesh['grp'=8,'dev'=32] {'grp','dev'}, use_global_device_ids=true, to_apply=%region_2.3 | all-reduce | flops 16 | bytes 128 | tf_op jit(solution)/shard_map/psum | solution.py:26
  240.4 0.0 copy-done
  240.4 0.1 convolution_bitcast_fusion
  240.5 0.1 dynamic_slice.3
  240.6 0.6 fusion.3
  241.2 0.0 all-gather.7.cloned.1.call-done
  241.2 17.5 %reshape.35 = bf16[8000,1280]{1,0:T(8,128)(2,1)} reshape(bf16[32,250,1280]{2,1,0:T(8,128)(2,1)} %all-gather.7.cloned.1.call-done) | data formatting | bytes 40960000
  258.7 15.0 %fusion = bf16[250,8000]{0,1:T(8,128)(2,1)} fusion(bf16[250,1280]{0,1:T(8,128)(2,1)S(1)} %bitcast.22, bf16[8000,1280]{1,0:T(8,128)(2,1)} %reshape.35, bf16[1,250,8000]{1,2,0:T(8,128)(2,1)} %copy.26, bf16[1,250,8000]{1,2,0:T(8,128)(2,1)} %copy.25, f32[]{:T(128)} %bitcast.5, f32[]{:T(128)} %bitcast.4), kind=kOutput, calls=%fused_computation.1 | convolution fusion | flops 5136000000 | bytes 33120008 | tf_op jit(solution)/shard_map/dot_general | solution.py:29
  273.7 0.0 copy-start.1
  273.7 54.6 %all_to_all.5 = bf16[250,8,1000]{0,2,1:T(8,128)(2,1)S(1)} all-to-all(bf16[250,8,1000]{0,2,1:T(8,128)(2,1)} %bitcast.20), channel_id=1, replica_groups=mesh['grp'=8,'dev'=32] {'grp'}, dimensions={1} | all-to-all | bytes 8000000 | tf_op jit(solution)/shard_map/all_to_all | solution.py:41
  328.3 0.7 convert_reduce_fusion
  329.1 0.0 copy-done.1
  329.1 1.2 add.19
  (2 shorter events, 0.0 us)
Async XLA Ops:
  6.5 233.8 %copy-start = (f32[16,16]{1,0:T(8,128)S(1)}, f32[16,16]{1,0:T(8,128)}, u32[]{:S(2)}) copy-start(f32[16,16]{1,0:T(8,128)} %param.7) | copy-start | bytes 3076
  6.5 79.7 %all-gather.5.cloned.1.call-start = ((), (), s32[]{:S(2)}) async-start(), calls=%async_computation.1 | async-start | bytes 10813440 | tf_op jit(solution)/shard_map/all_gather | solution.py:15
  7.3 233.9 %all-gather.7.cloned.1.call-start = ((), (), s32[]{:S(2)}) async-start(), calls=%async_computation.2 | async-start | bytes 21626880 | tf_op jit(solution)/shard_map/all_gather | solution.py:31
  273.7 55.4 %copy-start.1 = (f32[250,1000]{0,1:T(8,128)S(1)}, f32[250,1000]{0,1:T(8,128)}, u32[]{:S(2)}) copy-start(f32[250,1000]{0,1:T(8,128)} %param.6) | copy-start | bytes 3000004
Sparse Core Ops, SparseCore 0:
  9.2 77.0 all-gather.4
  111.0 121.1 all-gather.6

commit v3 on v2

--- a/solution.py
+++ b/solution.py
@@ -2,6 +2,8 @@
 import jax.numpy as jnp
 from jax import lax
 from jax.sharding import PartitionSpec as P
+
+TILE_ROWS = 256
 
 
 def shards(slab, orbitals, hcore, metric_inv):
@@ -26,9 +28,12 @@
     density_all = lax.psum(density_slots, ("grp", "dev")).reshape(group_count * aux_count)
     fit_coef = jnp.dot(metric_inv, density_all, precision=lax.Precision.HIGHEST)
     half_flat = jnp.transpose(half_done, (1, 0, 2)).reshape(row_count, aux_count * occ_count)
+    dev_count = full_width // row_count
+    tile = -(-row_count // TILE_ROWS) * TILE_ROWS
+    half_padded = jnp.pad(half_flat, ((0, tile - row_count), (0, 0)))
     exchange_part = lax.dot_general(
         half_flat,
-        lax.all_gather(half_flat, "dev", axis=0, tiled=True),
+        lax.all_gather(half_padded, "dev", axis=0, tiled=True),
         (((1,), (1,)), ((), ())),
         preferred_element_type=jnp.float32,
     )
@@ -36,10 +41,15 @@
     coulomb_part = jnp.zeros((row_count, full_width), jnp.float32)
     for aux_index in range(aux_count):
         coulomb_part = coulomb_part + local_coef[aux_index] * slab[aux_index].astype(jnp.float32)
+    coulomb_part = jnp.pad(
+        coulomb_part.reshape(row_count, dev_count, row_count), ((0, 0), (0, 0), (0, tile - row_count))
+    ).reshape(row_count, dev_count * tile)
     partial = (2.0 * coulomb_part - exchange_part).astype(jnp.bfloat16)
-    partial = partial.reshape(row_count, group_count, full_width // group_count)
+    partial = partial.reshape(row_count, group_count, dev_count * tile // group_count)
     pieces = lax.all_to_all(partial, "grp", 1, 1, tiled=True)
     reduced = jnp.sum(pieces.astype(jnp.float32), axis=1)
+    reduced = reduced.reshape(row_count, dev_count // group_count, tile)[:, :, :row_count]
+    reduced = reduced.reshape(row_count, full_width // group_count)
     fock = hcore + reduced
     return fock
 

time: 339 us -> 357 us (1.053); the launches traced: 337 us -> 350 us
  other arithmetic: 2.01 us -> 49.5 us
  local copies, waits for them, and re-layouts: 101 us -> 64.9 us
    add x0 -> x1, other arithmetic: none -> 39.2 us  [shards(): coulomb_part + local_coef[aux_index] * slab[aux_index].astype(jnp.float32)]
    unnamed x10 -> x13, local copies, waits for them, and re-layouts: 71.5 us -> 35.1 us
    slice x1 -> x0, local copies, waits for them, and re-layouts: 17.2 us -> none  [shards(): slab[aux_index].astype(jnp.float32)]
    add x0 -> x1, local copies, waits for them, and re-layouts: none -> 14 us  [shards(): coulomb_part + local_coef[aux_index] * slab[aux_index].astype(jnp.float32)]
    mul x0 -> x1, other arithmetic: none -> 4.39 us  [shards(): partial = (2.0 * coulomb_part - exchange_part).astype(jnp.bfloat16)]
    reduce_sum x1, other arithmetic: 0.74 us -> 4.69 us  [shards(): reduced = jnp.sum(pieces.astype(jnp.float32), axis=1)]
  transfers between devices with their start and end apart: 2 -> 2, of which waited for: 1 -> 1; matrix products, arithmetic and copies ran while one was open for 21% -> 25% of each run, Pallas kernels for 0% -> 0%
where the time goes in v3:
time: 357 us; the launch traced here: 350 us
  blocking collectives  132 us (37%)
  local copies, waits for them, and re-layouts  64.9 us (18%)
  waiting for transfers between devices  62 us (17%)
  other arithmetic  49.5 us (14%)
  matrix products  27.2 us (8%)
  between operations  14 us (4%)
    psum x1, blocking collectives, shards(): lax.psum(density_slots, ('grp', 'dev')).reshape(group_count * aux_count)  76 us
    all_gather x1, waiting for transfers between devices, shards(): lax.all_gather(orbitals, 'dev', axis=0, tiled=True)  61.2 us
    all_to_all x1, blocking collectives, shards(): pieces = lax.all_to_all(partial, 'grp', 1, 1, tiled=True)  56.2 us
    add x1, other arithmetic, shards(): coulomb_part + local_coef[aux_index] * slab[aux_index].astype(jnp.float32)  39.2 us
    unnamed x13, local copies, waits for them, and re-layouts  35.1 us
    dot_general x1, matrix products, shards(): lax.dot_general(half_flat, lax.all_gather(half_padded, 'dev', axis=0, til...  14.9 us
    add x1, local copies, waits for them, and re-layouts, shards(): coulomb_part + local_coef[aux_index] * slab[aux_index].astype(jnp.float32)  14 us
    dot_general x1, matrix products, shards(): jnp.dot(slab_flat, lax.all_gather(orbitals, 'dev', axis=0, tiled=True), p...  12.2 us
  transfers between devices with their start and end apart: 2, of which 1 were waited for; matrix products, arithmetic and copies ran while one was open for 25% of the time, Pallas kernels for 0%

profile of v3, /device:TPU:2, one launch (start us, length us, event | category | flops | bytes accessed | tf_op | source)
XLA Modules:
  0.0 349.8 jit_solution(883629794824704937)
XLA Ops:
  6.5 0.0 copy-start
  6.5 0.0 all-gather.6.cloned.1.call-start
  6.5 0.7 all-gather.6.cloned.1.call-update
  7.3 0.0 all-gather.4.cloned.1.call-start
  7.3 7.4 %copy.17 = bf16[2,250,8000]{2,1,0:T(8,128)(2,1)} copy(bf16[2,250,8000]{2,0,1:T(2,128)(2,1)} %param.4) | data formatting | bytes 16000000 | tf_op args[0]
  14.7 0.0 copy-start.2
  14.7 10.1 %reshape.37 = bf16[500,8000]{1,0:T(8,128)(2,1)} reshape(bf16[2,250,8000]{2,1,0:T(8,128)(2,1)} %copy.17) | data formatting | bytes 16000000 | tf_op jit(solution)/shard_map/reshape | solution.py:14
  24.8 0.0 copy-done.2
  24.8 0.1 mul.39
  24.9 0.1 mul.40
  25.0 61.2 %all-gather.6.cloned.1.call-done = bf16[32,250,640]{2,1,0:T(8,128)(2,1)} async-done(((bf16[1,250,640]{2,1,0:T(8,128)(2,1)}), bf16[32,250,640]{2,1,0:T(8,128)(2,1)}) %all-gather.6.cloned.1.call-update) | async-done | bytes 10240016 | tf_op jit(solution)/shard_map/all_gather | solution.py:17
  86.3 10.9 %reshape.45 = bf16[8000,640]{1,0:T(8,128)(2,1)} reshape(bf16[32,250,640]{2,1,0:T(8,128)(2,1)} %all-gather.6.cloned.1.call-done) | data formatting | bytes 20480000
  97.2 12.2 %multiply_reduce_fusion = (f32[500]{0:T(512)S(1)}, bf16[500,640]{1,0:T(8,128)(2,1)S(1)}) fusion(f32[500,640]{1,0:T(8,128)S(1)} %mul.40, bf16[500,8000]{1,0:T(8,128)(2,1)} %reshape.37, bf16[8000,640]{1,0:T(8,128)(2,1)} %reshape.45), kind=kOutput, calls=%fused_computation.6 | convolution fusion | flops 5121279488 | bytes 20162000 | tf_op jit(solution)/shard_map/dot_general | solution.py:15
  109.4 0.1 reshape.39
  109.5 0.3 copy.18
  109.8 1.0 pad.9
  110.8 0.0 all-gather.4.cloned.1.call-update
  110.8 0.1 reduce_sum.26
  110.9 0.1 reduce_sum.27
  111.0 0.1 reshape.38
  111.1 76.0 %psum.7 = f32[16]{0:T(128)S(1)} all-reduce(f32[16]{0:T(128)S(1)} %reshape.38), channel_id=1, replica_groups=mesh['grp'=8,'dev'=32] {'grp','dev'}, use_global_device_ids=true, to_apply=%region_2.3 | all-reduce | flops 16 | bytes 128 | tf_op jit(solution)/shard_map/psum | solution.py:28
  187.1 0.0 copy-done
  187.1 0.1 convolution_bitcast_fusion
  187.2 0.1 dynamic_slice.3
  187.3 0.6 fusion.2
  187.9 39.2 %add_reduce_fusion = f32[250,8000]{1,0:T(8,128)} fusion(bf16[2,250,8000]{2,0,1:T(2,128)(2,1)} %param.4, f32[]{:T(128)} %bitcast.5, f32[]{:T(128)} %bitcast.4), kind=kLoop, calls=%fused_computation.4 | loop fusion | flops 10000000 | bytes 16000008 | tf_op jit(solution)/shard_map/add | solution.py:43
  227.1 14.0 %add.26 = f32[250,32,250]{2,1,0:T(8,128)} reshape(f32[250,8000]{1,0:T(8,128)} %add_reduce_fusion) | data formatting | bytes 16000000 | tf_op jit(solution)/shard_map/add | solution.py:43
  241.2 4.4 %pad_multiply_fusion = f32[250,32,256]{2,1,0:T(8,128)S(1)} fusion(f32[250,32,250]{2,1,0:T(8,128)} %add.26), kind=kLoop, calls=%fused_computation.3 | loop fusion | flops 2048000 | bytes 16192000 | tf_op jit(solution)/shard_map/mul | solution.py:47
  245.6 1.6 pad.10
  247.2 10.8 %copy.23 = f32[32,8,32,256]{3,1,2,0:T(8,128)} copy(f32[32,8,32,256]{3,2,1,0:T(8,128)S(1)} %bitcast.26) | data formatting | bytes 16777216
  258.0 0.0 all-gather.4.cloned.1.call-done
  258.0 14.9 %fusion = bf16[250,8192]{1,0:T(8,128)(2,1)S(1)} fusion(f32[250,8192]{1,0:T(8,128)} %bitcast.27, bf16[250,1280]{0,1:T(8,128)(2,1)S(1)} %bitcast.31, bf16[8192,1280]{0,1:T(8,128)(2,1)} %all-gather.4.cloned.1.call-done), kind=kOutput, calls=%fused_computation.1 | convolution fusion | flops 5246976000 | bytes 33899520 | tf_op jit(solution)/shard_map/dot_general | solution.py:34
  272.9 4.3 %copy.24 = bf16[32,8,8,1024]{3,2,1,0:T(8,128)(2,1)S(1)} copy(bf16[32,8,8,1024]{3,1,2,0:T(8,128)(2,1)S(1)} %bitcast.28) | data formatting | bytes 8388608
  277.3 0.4 slice.21
  277.7 2.3 copy.19
  280.0 0.0 copy-start.3
  280.0 0.0 copy-start.1
  280.0 56.2 %all_to_all.5 = bf16[250,8,1024]{2,0,1:T(8,128)(2,1)S(1)} all-to-all(bf16[250,8,1024]{2,0,1:T(8,128)(2,1)S(1)} %copy.19), channel_id=1, replica_groups=mesh['grp'=8,'dev'=32] {'grp'}, dimensions={1} | all-to-all | bytes 8192000 | tf_op jit(solution)/shard_map/all_to_all | solution.py:49
  336.2 4.7 %convert_reduce_fusion = f32[250,1024]{1,0:T(8,128)S(1)} fusion(bf16[250,8,1024]{2,0,1:T(8,128)(2,1)S(1)} %all_to_all.5), kind=kLoop, calls=%fused_computation.2 | loop fusion | flops 3840000 | bytes 5120000 | tf_op jit(solution)/shard_map/reduce_sum | solution.py:50
  340.9 0.3 copy.22
  341.3 0.1 reshape.43
  341.4 0.0 copy-done.3
  341.4 1.1 add.27
  342.5 0.0 copy-done.1
  (2 shorter events, 0.0 us)
Async XLA Ops:
  6.5 180.6 %copy-start = (f32[16,16]{1,0:T(8,128)S(1)}, f32[16,16]{1,0:T(8,128)}, u32[]{:S(2)}) copy-start(f32[16,16]{1,0:T(8,128)} %param.7) | copy-start | bytes 3076
  6.5 79.7 %all-gather.6.cloned.1.call-start = ((), (), s32[]{:S(2)}) async-start(), calls=%async_computation.2 | async-start | bytes 10813440 | tf_op jit(solution)/shard_map/all_gather | solution.py:17
  7.3 250.8 %all-gather.4.cloned.1.call-start = ((), (), s32[]{:S(2)}) async-start(), calls=%async_computation.1 | async-start | bytes 21626880 | tf_op jit(solution)/shard_map/all_gather | solution.py:36
  14.7 10.1 %copy-start.2 = (bf16[250,640]{1,0:T(8,128)(2,1)S(1)}, bf16[250,640]{1,0:T(8,128)(2,1)}, u32[]{:S(2)}) copy-start(bf16[250,640]{1,0:T(8,128)(2,1)} %param.5) | copy-start | bytes 960004
  280.0 61.4 %copy-start.3 = (f32[250,1000]{0,1:T(8,128)S(1)}, f32[250,1000]{0,1:T(8,128)}, u32[]{:S(2)}) copy-start(f32[250,1000]{0,1:T(8,128)} %param.6) | copy-start | bytes 3000004
  280.0 62.5 %copy-start.1 = (f32[16,16]{1,0:T(8,128)S(1)}, f32[16,16]{1,0:T(8,128)}, u32[]{:S(2)}) copy-start(f32[16,16]{1,0:T(8,128)} %param.7) | copy-start | bytes 3076
Sparse Core Ops, SparseCore 0:
  9.2 77.0 all-gather.5
  110.9 144.1 all-gather.3

commit v4 on v1

--- a/solution.py
+++ b/solution.py
@@ -2,6 +2,7 @@
 import jax.numpy as jnp
 from jax import lax
 from jax.sharding import PartitionSpec as P
+from jax.experimental.layout import Layout, with_layout_constraint
 
 
 def shards(slab, orbitals, hcore, metric_inv):
@@ -36,6 +37,7 @@
         coulomb_part = coulomb_part + local_coef[aux_index] * slab[aux_index].astype(jnp.float32)
     group_count = lax.psum(1, "grp")
     partial = (2.0 * coulomb_part - exchange_part).astype(jnp.bfloat16)
+    partial = with_layout_constraint(partial, Layout((0, 1)))
     partial = partial.reshape(row_count, group_count, full_width // group_count)
     pieces = lax.all_to_all(partial, "grp", 1, 1, tiled=True)
     reduced = jnp.sum(pieces.astype(jnp.float32), axis=1)

time: 336 us -> 338 us (level)
  local copies, waits for them, and re-layouts: 102 us -> 56.6 us
  waiting for transfers between devices: 61 us -> 102 us
  blocking collectives: 125 us -> 134 us
    all_gather x1, waiting for transfers between devices: 0.01 us -> 41 us  [shards(): lax.all_gather(half_flat, 'dev', axis=0, tiled=True)]
    unnamed x15, local copies, waits for them, and re-layouts: 72.4 us -> 37.7 us
    slice x1 -> x0, local copies, waits for them, and re-layouts: 17.2 us -> none  [shards(): slab[aux_index].astype(jnp.float32)]
    all_to_all x1, blocking collectives: 48.6 us -> 56.5 us  [shards(): pieces = lax.all_to_all(partial, 'grp', 1, 1, tiled=True)]
    another operation x0 -> x1, local copies, waits for them, and re-layouts: none -> 6.46 us  [shards(): partial = with_layout_constraint(partial, Layout((0, 1)))]
  transfers between devices with their start and end apart: 2 -> 2, of which waited for: 1 -> 2; matrix products, arithmetic and copies ran while one was open for 22% -> 6% of each run, Pallas kernels for 0% -> 0%
where the time goes in v4:
time: 338 us; the launch traced here: 336 us
  blocking collectives  134 us (40%)
  waiting for transfers between devices  102 us (30%)
  local copies, waits for them, and re-layouts  56.6 us (17%)
  matrix products  27.3 us (8%)
  between operations  14.1 us (4%)
    all_gather x1, waiting for transfers between devices, shards(): lax.all_gather(orbitals, 'dev', axis=0, tiled=True)  60.4 us
    all_to_all x1, blocking collectives, shards(): pieces = lax.all_to_all(partial, 'grp', 1, 1, tiled=True)  56.5 us
    psum x1, blocking collectives, shards(): group_density = lax.psum(aux_density, 'dev')  52.6 us
    all_gather x1, waiting for transfers between devices, shards(): lax.all_gather(half_flat, 'dev', axis=0, tiled=True)  41 us
    unnamed x15, local copies, waits for them, and re-layouts  37.7 us
    unnamed x1, blocking collectives  24.5 us
    dot_general x1, matrix products, shards(): lax.dot_general(half_flat, lax.all_gather(half_flat, 'dev', axis=0, tiled...  14.9 us
    dot_general x1, matrix products, shards(): jnp.dot(slab_flat, lax.all_gather(orbitals, 'dev', axis=0, tiled=True), p...  12.2 us
  transfers between devices with their start and end apart: 2, of which 2 were waited for; matrix products, arithmetic and copies ran while one was open for 6% of the time, Pallas kernels for 0%

profile of v4, /device:TPU:2, one launch (start us, length us, event | category | flops | bytes accessed | tf_op | source)
XLA Modules:
  0.0 335.6 jit_solution(5033810884826568014)
XLA Ops:
  6.5 0.0 copy-start
  6.5 0.0 all-gather.5.cloned.1.call-start
  6.5 0.7 all-gather.5.cloned.1.call-update
  7.3 0.0 all-gather.7.cloned.1.call-start
  7.3 1.1 mul.37
  8.4 0.1 mul.38
  8.5 7.3 %copy.21 = bf16[2,250,8000]{2,1,0:T(8,128)(2,1)} copy(bf16[2,250,8000]{2,0,1:T(2,128)(2,1)} %param.4) | data formatting | bytes 16000000 | tf_op args[0]
  15.8 10.1 %reshape.24 = bf16[500,8000]{1,0:T(8,128)(2,1)} reshape(bf16[2,250,8000]{2,1,0:T(8,128)(2,1)} %copy.21) | data formatting | bytes 16000000 | tf_op jit(solution)/shard_map/reshape | solution.py:13
  25.9 60.4 %all-gather.5.cloned.1.call-done = bf16[32,250,640]{2,1,0:T(8,128)(2,1)} async-done(((bf16[1,250,640]{2,1,0:T(8,128)(2,1)}), bf16[32,250,640]{2,1,0:T(8,128)(2,1)}) %all-gather.5.cloned.1.call-update) | async-done | bytes 10240016 | tf_op jit(solution)/shard_map/all_gather | solution.py:16
  86.3 10.9 %reshape.32 = bf16[8000,640]{1,0:T(8,128)(2,1)} reshape(bf16[32,250,640]{2,1,0:T(8,128)(2,1)} %all-gather.5.cloned.1.call-done) | data formatting | bytes 20480000
  97.2 0.0 copy-start.3
  97.2 12.2 %multiply_reduce_fusion = (f32[500]{0:T(512)S(1)}, bf16[500,640]{1,0:T(8,128)(2,1)S(1)}) fusion(f32[500,640]{1,0:T(8,128)S(1)} %mul.38, bf16[500,8000]{1,0:T(8,128)(2,1)} %reshape.24, bf16[8000,640]{1,0:T(8,128)(2,1)} %reshape.32), kind=kOutput, calls=%fused_computation.4 | convolution fusion | flops 5121279488 | bytes 20162000 | tf_op jit(solution)/shard_map/dot_general | solution.py:14
  109.4 0.1 reshape.25
  109.6 0.3 copy.24
  109.8 1.1 copy.26
  110.9 0.0 all-gather.7.cloned.1.call-update
  110.9 0.0 copy-done.3
  110.9 0.6 dynamic-slice.1
  111.6 0.1 reduce_sum.26
  111.6 0.1 reduce_sum.27
  112.4 52.6 %psum.7 = f32[2]{0:T(128)S(1)} all-reduce(f32[2]{0:T(128)S(1)} %reduce_sum.27), channel_id=1, replica_groups=mesh['grp'=8,'dev'=32] {'dev'}, use_global_device_ids=true, to_apply=%region_2.0 | all-reduce | flops 2 | bytes 16 | tf_op jit(solution)/shard_map/psum | solution.py:24
  164.9 0.2 dynamic-update-slice
  165.2 24.5 %all-reduce = f32[16]{0:T(128)S(1)} all-reduce(f32[16]{0:T(128)S(1)} %dynamic-update-slice), channel_id=1, replica_groups=mesh['grp'=8,'dev'=32] {'grp'}, use_global_device_ids=true, to_apply=%add | all-reduce | flops 16 | bytes 128
  189.7 0.0 copy-done
  189.7 0.1 convolution_bitcast_fusion
  189.8 0.1 dynamic_slice.3
  189.9 0.6 fusion.2
  190.5 41.0 %all-gather.7.cloned.1.call-done = bf16[32,250,1280]{2,1,0:T(8,128)(2,1)} async-done(((bf16[1,250,1280]{2,1,0:T(8,128)(2,1)}), bf16[32,250,1280]{2,1,0:T(8,128)(2,1)}) %all-gather.7.cloned.1.call-update) | async-done | bytes 20480016 | tf_op jit(solution)/shard_map/all_gather | solution.py:30
  231.5 17.5 %reshape.34 = bf16[8000,1280]{1,0:T(8,128)(2,1)} reshape(bf16[32,250,1280]{2,1,0:T(8,128)(2,1)} %all-gather.7.cloned.1.call-done) | data formatting | bytes 40960000
  249.0 14.9 %fusion = bf16[250,8000]{1,0:T(8,128)(2,1)} fusion(bf16[250,1280]{0,1:T(8,128)(2,1)S(1)} %bitcast.22, bf16[8000,1280]{1,0:T(8,128)(2,1)} %reshape.34, bf16[2,250,8000]{2,1,0:T(8,128)(2,1)} %copy.21, f32[]{:T(128)} %bitcast.5, f32[]{:T(128)} %bitcast.4), kind=kOutput, calls=%fused_computation.1 | convolution fusion | flops 5136000000 | bytes 33120008 | tf_op jit(solution)/shard_map/dot_general | solution.py:28
  263.9 0.0 copy-start.1
  263.9 6.5 %copy.27 = bf16[250,8000]{0,1:T(8,128)(2,1)} copy(bf16[250,8000]{1,0:T(8,128)(2,1)} %fusion) | data formatting | bytes 8000000 | tf_op jit(solution)/shard_map/layout_constraint | solution.py:40
  270.4 0.0 copy-start.2
  270.4 56.5 %all_to_all.5 = bf16[250,8,1000]{0,2,1:T(8,128)(2,1)S(1)} all-to-all(bf16[250,8,1000]{0,2,1:T(8,128)(2,1)} %bitcast.20), channel_id=1, replica_groups=mesh['grp'=8,'dev'=32] {'grp'}, dimensions={1} | all-to-all | bytes 8000000 | tf_op jit(solution)/shard_map/all_to_all | solution.py:42
  326.9 0.7 convert_reduce_fusion
  327.6 0.0 copy-done.2
  327.6 1.2 add.14
  328.8 0.0 copy-done.1
  (1 shorter events, 0.0 us)
Async XLA Ops:
  6.5 183.2 %copy-start = (f32[16,16]{1,0:T(8,128)S(1)}, f32[16,16]{1,0:T(8,128)}, u32[]{:S(2)}) copy-start(f32[16,16]{1,0:T(8,128)} %param.7) | copy-start | bytes 3076
  6.5 79.7 %all-gather.5.cloned.1.call-start = ((), (), s32[]{:S(2)}) async-start(), calls=%async_computation.1 | async-start | bytes 10813440 | tf_op jit(solution)/shard_map/all_gather | solution.py:16
  7.3 224.2 %all-gather.7.cloned.1.call-start = ((), (), s32[]{:S(2)}) async-start(), calls=%async_computation.2 | async-start | bytes 21626880 | tf_op jit(solution)/shard_map/all_gather | solution.py:30
  97.2 13.7 %copy-start.3 = (u32[256]{0:T(256)S(1)}, u32[256]{0:T(256)}, u32[]{:S(2)}) copy-start(u32[256]{0:T(256)} %constant.21) | copy-start | bytes 3076
  263.9 64.8 %copy-start.1 = (f32[16,16]{1,0:T(8,128)S(1)}, f32[16,16]{1,0:T(8,128)}, u32[]{:S(2)}) copy-start(f32[16,16]{1,0:T(8,128)} %param.7) | copy-start | bytes 3076
  270.4 57.2 %copy-start.2 = (f32[250,1000]{0,1:T(8,128)S(1)}, f32[250,1000]{0,1:T(8,128)}, u32[]{:S(2)}) copy-start(f32[250,1000]{0,1:T(8,128)} %param.6) | copy-start | bytes 3000004
Sparse Core Ops, SparseCore 0:
  9.2 77.0 all-gather.4
  111.0 120.4 all-gather.6

commit v5 on v0

--- a/solution.py
+++ b/solution.py
@@ -2,6 +2,8 @@
 import jax.numpy as jnp
 from jax import lax
 from jax.sharding import PartitionSpec as P
+
+TILE_ROWS = 256
 
 
 def shards(slab, orbitals, hcore, metric_inv):
@@ -24,18 +26,32 @@
     density_all = lax.all_gather(group_density, "grp", axis=0, tiled=True)
     fit_coef = jnp.dot(metric_inv, density_all, precision=lax.Precision.HIGHEST)
     half_flat = jnp.transpose(half_done, (1, 0, 2)).reshape(row_count, aux_count * occ_count)
-    exchange_part = lax.dot_general(
-        half_flat,
-        lax.all_gather(half_flat, "dev", axis=0, tiled=True),
-        (((1,), (1,)), ((), ())),
-        preferred_element_type=jnp.float32,
-    )
+    dev_count = full_width // row_count
+    group_count = lax.psum(1, "grp")
+    tile = -(-row_count // TILE_ROWS) * TILE_ROWS
     local_coef = lax.dynamic_slice_in_dim(fit_coef, group_index * aux_count, aux_count)
     coulomb_part = jnp.zeros((row_count, full_width), jnp.float32)
     for aux_index in range(aux_count):
         coulomb_part = coulomb_part + local_coef[aux_index] * slab[aux_index].astype(jnp.float32)
-    reduced = lax.psum_scatter(
-        2.0 * coulomb_part - exchange_part, "grp", scatter_dimension=1, tiled=True
+    coulomb_pieces = lax.all_to_all(
+        (2.0 * coulomb_part).astype(jnp.bfloat16).reshape(row_count, group_count, full_width // group_count),
+        "grp", 1, 1, tiled=True,
+    )
+    half_padded = jnp.pad(half_flat, ((0, tile - row_count), (0, 0)))
+    exchange_part = lax.dot_general(
+        half_flat,
+        lax.all_gather(half_padded, "dev", axis=0, tiled=True),
+        (((1,), (1,)), ((), ())),
+        preferred_element_type=jnp.float32,
+    )
+    exchange_pieces = lax.all_to_all(
+        exchange_part.astype(jnp.bfloat16).reshape(row_count, group_count, dev_count * tile // group_count),
+        "grp", 1, 1, tiled=True,
+    )
+    exchange_sum = jnp.sum(exchange_pieces.astype(jnp.float32), axis=1)
+    exchange_sum = exchange_sum.reshape(row_count, dev_count // group_count, tile)[:, :, :row_count]
+    reduced = jnp.sum(coulomb_pieces.astype(jnp.float32), axis=1) - exchange_sum.reshape(
+        row_count, full_width // group_count
     )
     fock = hcore + reduced
     return fock

time: 405 us -> 374 us (0.923); the launches traced: 403 us -> 367 us
  waiting for transfers between devices: 180 us -> 127 us
  other arithmetic: 2.49 us -> 20.8 us
  starting transfers between devices: 0.08 us -> 9.61 us
  local copies, waits for them, and re-layouts: 102 us -> 93.6 us
    reduce_scatter x1 -> x0, waiting for transfers between devices: 119 us -> none  [shards(): lax.psum_scatter(2.0 * coulomb_part - exchange_part, 'grp', scatter_dimen...]
    all_to_all x0 -> x2, waiting for transfers between devices: none -> 65.9 us  [the longest x1 46 us: shards(): lax.all_to_all(exchange_part.astype(jnp.bfloat16).reshape(row_count, grou...]
    unnamed x15 -> x12, local copies, waits for them, and re-layouts: 72.3 us -> 58.1 us
    reduce_sum x0 -> x2, other arithmetic: none -> 9.9 us  [the longest x1 6.91 us: shards(): exchange_sum = jnp.sum(exchange_pieces.astype(jnp.float32), axis=1)]
    all_to_all x0 -> x2, starting transfers between devices: none -> 9.57 us  [the longest x1 4.8 us: shards(): lax.all_to_all((2.0 * coulomb_part).astype(jnp.bfloat16).reshape(row_coun...]
    another operation x0 -> x1, other arithmetic: none -> 8.3 us
    reshape x0 -> x4, local copies, waits for them, and re-layouts: none -> 5.07 us  [the longest x2 4.62 us: shards(): exchange_part.astype(jnp.bfloat16)]
  transfers between devices with their start and end apart: 3 -> 4, of which waited for: 2 -> 3; matrix products, arithmetic and copies ran while one was open for 18% -> 29% of each run, Pallas kernels for 0% -> 0%
where the time goes in v5:
time: 374 us; the launch traced here: 367 us
  waiting for transfers between devices  127 us (34%)
  local copies, waits for them, and re-layouts  93.6 us (25%)
  blocking collectives  76.3 us (20%)
  matrix products  25.5 us (7%)
  other arithmetic  20.8 us (6%)
  between operations  14.2 us (4%)
  starting transfers between devices  9.61 us (3%)
    all_gather x1, waiting for transfers between devices, shards(): lax.all_gather(orbitals, 'dev', axis=0, tiled=True)  60.3 us
    unnamed x12, local copies, waits for them, and re-layouts  58.1 us
    psum x1, blocking collectives, shards(): group_density = lax.psum(aux_density, 'dev')  52.5 us
    all_to_all x1, waiting for transfers between devices, shards(): lax.all_to_all(exchange_part.astype(jnp.bfloat16).reshape(row_count, grou...  46 us
    unnamed x1, blocking collectives  23.9 us
    all_to_all x1, waiting for transfers between devices, shards(): lax.all_to_all((2.0 * coulomb_part).astype(jnp.bfloat16).reshape(row_coun...  19.8 us
    slice x1, local copies, waits for them, and re-layouts, shards(): slab[aux_index].astype(jnp.float32)  17 us
    dot_general x1, matrix products, shards(): lax.dot_general(half_flat, lax.all_gather(half_padded, 'dev', axis=0, til...  13.2 us
  transfers between devices with their start and end apart: 4, of which 3 were waited for; matrix products, arithmetic and copies ran while one was open for 29% of the time, Pallas kernels for 0%

profile of v5, /device:TPU:2, one launch (start us, length us, event | category | flops | bytes accessed | tf_op | source)
XLA Modules:
  0.0 366.8 jit_solution(1207774624756197913)
XLA Ops:
  6.5 0.0 copy-start
  6.5 0.0 all-gather.6.cloned.1.call-start
  6.5 0.7 all-gather.6.cloned.1.call-update
  7.3 0.0 all-gather.4.cloned.1.call-start
  7.3 1.1 mul.40
  8.4 0.1 mul.41
  8.5 7.4 %copy.23 = bf16[2,250,8000]{2,1,0:T(8,128)(2,1)} copy(bf16[2,250,8000]{2,0,1:T(2,128)(2,1)} %param.4) | data formatting | bytes 16000000 | tf_op args[0]
  15.9 10.1 %reshape.34 = bf16[500,8000]{1,0:T(8,128)(2,1)} reshape(bf16[2,250,8000]{2,1,0:T(8,128)(2,1)} %copy.23) | data formatting | bytes 16000000 | tf_op jit(solution)/shard_map/reshape | solution.py:14
  25.9 60.3 %all-gather.6.cloned.1.call-done = bf16[32,250,640]{2,1,0:T(8,128)(2,1)} async-done(((bf16[1,250,640]{2,1,0:T(8,128)(2,1)}), bf16[32,250,640]{2,1,0:T(8,128)(2,1)}) %all-gather.6.cloned.1.call-update) | async-done | bytes 10240016 | tf_op jit(solution)/shard_map/all_gather | solution.py:17
  86.3 10.9 %reshape.44 = bf16[8000,640]{1,0:T(8,128)(2,1)} reshape(bf16[32,250,640]{2,1,0:T(8,128)(2,1)} %all-gather.6.cloned.1.call-done) | data formatting | bytes 20480000
  97.2 12.2 %multiply_reduce_fusion = (f32[500]{0:T(512)S(1)}, bf16[500,640]{1,0:T(8,128)(2,1)S(1)}) fusion(f32[500,640]{1,0:T(8,128)S(1)} %mul.41, bf16[500,8000]{1,0:T(8,128)(2,1)} %reshape.34, bf16[8000,640]{1,0:T(8,128)(2,1)} %reshape.44), kind=kOutput, calls=%fused_computation.5 | convolution fusion | flops 5121279488 | bytes 20162000 | tf_op jit(solution)/shard_map/dot_general | solution.py:15
  109.4 0.1 reshape.35
  109.5 0.3 copy.26
  109.8 1.0 pad.4
  110.8 0.0 all-gather.4.cloned.1.call-update
  110.8 17.0 %fusion.1 = (bf16[1,250,8000]{2,0,1:T(2,128)(2,1)}, bf16[1,250,8000]{2,0,1:T(2,128)(2,1)}) fusion(bf16[2,250,8000]{2,0,1:T(2,128)(2,1)} %param.4), kind=kLoop, calls=%fused_computation.9 | loop fusion | bytes 16000000 | tf_op jit(solution)/shard_map/slice | solution.py:35
  127.8 17.3 %copy.31 = bf16[1,250,8000]{1,2,0:T(8,128)(2,1)} copy(bf16[1,250,8000]{2,0,1:T(2,128)(2,1)} %get-tuple-element.5) | data formatting | bytes 8000000
  145.1 0.0 copy-start.1
  145.1 17.3 %copy.32 = bf16[1,250,8000]{1,2,0:T(8,128)(2,1)} copy(bf16[1,250,8000]{2,0,1:T(2,128)(2,1)} %get-tuple-element.6) | data formatting | bytes 8000000
  162.4 0.0 copy-done.1
  162.4 0.6 dynamic-slice.1
  163.0 0.1 reduce_sum.35
  163.1 0.1 reduce_sum.36
  163.9 52.5 %psum.7 = f32[2]{0:T(128)S(1)} all-reduce(f32[2]{0:T(128)S(1)} %reduce_sum.36), channel_id=1, replica_groups=mesh['grp'=8,'dev'=32] {'dev'}, use_global_device_ids=true, to_apply=%region_2.3 | all-reduce | flops 2 | bytes 16 | tf_op jit(solution)/shard_map/psum | solution.py:25
  216.3 0.2 dynamic-update-slice
  216.5 23.9 %all-reduce.1 = f32[16]{0:T(128)S(1)} all-reduce(f32[16]{0:T(128)S(1)} %dynamic-update-slice), channel_id=1, replica_groups=mesh['grp'=8,'dev'=32] {'grp'}, use_global_device_ids=true, to_apply=%add.1 | all-reduce | flops 16 | bytes 128
  240.4 0.0 copy-done
  240.4 0.1 convolution_bitcast_fusion
  240.5 0.1 dynamic_slice.3
  240.6 0.7 fusion.2
  241.3 8.3 %multiply_convert_fusion = bf16[1,250,8000]{1,2,0:T(8,128)(2,1)} fusion(bf16[1,250,8000]{1,2,0:T(8,128)(2,1)} %copy.32, bf16[1,250,8000]{1,2,0:T(8,128)(2,1)} %copy.31, f32[]{:T(128)} %bitcast.5, f32[]{:T(128)} %bitcast.4), kind=kLoop, calls=%fused_computation.3 | loop fusion | flops 14000000 | bytes 12000008 | tf_op jit(solution)/shard_map/convert
  249.6 4.8 %all-to-all-start = ((bf16[250,8,1000]{0,2,1:T(8,128)(2,1)}), bf16[250,8,1000]{0,2,1:T(8,128)(2,1)}, u32[]{:S(2)}, u32[]{:S(2)}) async-start(bf16[250,8,1000]{0,2,1:T(8,128)(2,1)} %bitcast.26), calls=%async_computation | async-start | bytes 8192000 | tf_op jit(solution)/shard_map/all_to_all | solution.py:36
  254.4 0.0 all-gather.4.cloned.1.call-done
  254.4 13.2 %convolution_convert_fusion = bf16[250,8192]{1,0:T(8,128)(2,1)S(1)} fusion(bf16[250,1280]{0,1:T(8,128)(2,1)S(1)} %bitcast.28, bf16[8192,1280]{0,1:T(8,128)(2,1)} %all-gather.4.cloned.1.call-done), kind=kOutput, calls=%fused_computation | convolution fusion | flops 5244928000 | bytes 25707520 | tf_op jit(solution)/shard_map/dot_general | solution.py:41
  267.6 4.3 %copy.33 = bf16[32,8,8,1024]{3,2,1,0:T(8,128)(2,1)S(1)} copy(bf16[32,8,8,1024]{3,1,2,0:T(8,128)(2,1)S(1)} %bitcast.24) | data formatting | bytes 8388608
  271.9 0.4 slice.21
  272.4 4.2 %copy.27 = bf16[250,8,1024]{2,0,1:T(8,128)(2,1)} copy(bf16[250,8,1024]{2,1,0:T(8,128)(2,1)S(1)} %slice.21) | data formatting | bytes 8192000 | tf_op jit(solution)/shard_map/reshape | solution.py:48
  276.6 19.8 %all-to-all-done = bf16[250,8,1000]{0,2,1:T(8,128)(2,1)} async-done(((bf16[250,8,1000]{0,2,1:T(8,128)(2,1)}), bf16[250,8,1000]{0,2,1:T(8,128)(2,1)}, u32[]{:S(2)}, u32[]{:S(2)}) %all-to-all-start) | async-done | bytes 4000032 | tf_op jit(solution)/shard_map/all_to_all | solution.py:36
  296.4 4.8 %all-to-all-start.1 = ((bf16[250,8,1024]{2,0,1:T(8,128)(2,1)}), bf16[250,8,1024]{2,0,1:T(8,128)(2,1)}, u32[]{:S(2)}, u32[]{:S(2)}) async-start(bf16[250,8,1024]{2,0,1:T(8,128)(2,1)} %copy.27), calls=%async_computation.1 | async-start | bytes 8388608 | tf_op jit(solution)/shard_map/all_to_all | solution.py:47
  301.2 3.0 convert_reduce_fusion.1
  304.2 46.0 %all-to-all-done.1 = bf16[250,8,1024]{2,0,1:T(8,128)(2,1)} async-done(((bf16[250,8,1024]{2,0,1:T(8,128)(2,1)}), bf16[250,8,1024]{2,0,1:T(8,128)(2,1)}, u32[]{:S(2)}, u32[]{:S(2)}) %all-to-all-start.1) | async-done | bytes 4096032 | tf_op jit(solution)/shard_map/all_to_all | solution.py:47
  350.2 6.9 %convert_reduce_fusion = f32[250,1024]{1,0:T(8,128)S(1)} fusion(bf16[250,8,1024]{2,0,1:T(8,128)(2,1)} %all-to-all-done.1), kind=kLoop, calls=%fused_computation.1 | loop fusion | flops 3840000 | bytes 5120000 | tf_op jit(solution)/shard_map/reduce_sum | solution.py:51
  357.1 0.3 copy.30
  357.4 0.1 reshape.39
  357.6 2.4 subtract_add_fusion
  (1 shorter events, 0.0 us)
Async XLA Ops:
  6.5 233.9 %copy-start = (f32[16,16]{1,0:T(8,128)S(1)}, f32[16,16]{1,0:T(8,128)}, u32[]{:S(2)}) copy-start(f32[16,16]{1,0:T(8,128)} %param.7) | copy-start | bytes 3076
  6.5 79.7 %all-gather.6.cloned.1.call-start = ((), (), s32[]{:S(2)}) async-start(), calls=%async_computation.3 | async-start | bytes 10813440 | tf_op jit(solution)/shard_map/all_gather | solution.py:17
  7.3 247.1 %all-gather.4.cloned.1.call-start = ((), (), s32[]{:S(2)}) async-start(), calls=%async_computation.2 | async-start | bytes 21626880 | tf_op jit(solution)/shard_map/all_gather | solution.py:43
  145.1 17.3 %copy-start.1 = (u32[256]{0:T(256)S(1)}, u32[256]{0:T(256)}, u32[]{:S(2)}) copy-start(u32[256]{0:T(256)} %constant.25) | copy-start | bytes 3076
  249.6 46.8 %all-to-all-start = ((bf16[250,8,1000]{0,2,1:T(8,128)(2,1)}), bf16[250,8,1000]{0,2,1:T(8,128)(2,1)}, u32[]{:S(2)}, u32[]{:S(2)}) async-start(bf16[250,8,1000]{0,2,1:T(8,128)(2,1)} %bitcast.26), calls=%async_computation | async-start | bytes 8192000 | tf_op jit(solution)/shard_map/all_to_all | solution.py:36
  296.4 53.8 %all-to-all-start.1 = ((bf16[250,8,1024]{2,0,1:T(8,128)(2,1)}), bf16[250,8,1024]{2,0,1:T(8,128)(2,1)}, u32[]{:S(2)}, u32[]{:S(2)}) async-start(bf16[250,8,1024]{2,0,1:T(8,128)(2,1)} %copy.27), calls=%async_computation.1 | async-start | bytes 8388608 | tf_op jit(solution)/shard_map/all_to_all | solution.py:47
Sparse Core Ops, SparseCore 0:
  9.2 77.0 all-gather.5
  110.9 142.6 all-gather.3

commit v6 on v5

--- a/solution.py
+++ b/solution.py
@@ -2,6 +2,7 @@
 import jax.numpy as jnp
 from jax import lax
 from jax.sharding import PartitionSpec as P
+from jax.experimental.layout import Layout, with_layout_constraint
 
 TILE_ROWS = 256
 
@@ -33,8 +34,9 @@
     coulomb_part = jnp.zeros((row_count, full_width), jnp.float32)
     for aux_index in range(aux_count):
         coulomb_part = coulomb_part + local_coef[aux_index] * slab[aux_index].astype(jnp.float32)
+    coulomb_sent = with_layout_constraint((2.0 * coulomb_part).astype(jnp.bfloat16), Layout((0, 1)))
     coulomb_pieces = lax.all_to_all(
-        (2.0 * coulomb_part).astype(jnp.bfloat16).reshape(row_count, group_count, full_width // group_count),
+        coulomb_sent.reshape(row_count, group_count, full_width // group_count),
         "grp", 1, 1, tiled=True,
     )
     half_padded = jnp.pad(half_flat, ((0, tile - row_count), (0, 0)))

time: 374 us -> 381 us (1.019)
  waiting for transfers between devices: 127 us -> 182 us
  local copies, waits for them, and re-layouts: 93.6 us -> 48.3 us
    all_gather x1, waiting for transfers between devices: 0.02 us -> 74.9 us  [shards(): lax.all_gather(half_padded, 'dev', axis=0, tiled=True)]
    unnamed x12, local copies, waits for them, and re-layouts: 58.1 us -> 23.4 us
    all_to_all x1, waiting for transfers between devices: 19.8 us -> 0.01 us  [shards(): lax.all_to_all(coulomb_sent.reshape(row_count, group_count, full_width //...]
    slice x1 -> x0, local copies, waits for them, and re-layouts: 17 us -> none  [shards(): slab[aux_index].astype(jnp.float32)]
    another operation x1 -> x0, other arithmetic: 8.3 us -> none
    mul x0 -> x1, other arithmetic: none -> 7.24 us  [shards(): 2.0 * coulomb_part]
    another operation x0 -> x1, local copies, waits for them, and re-layouts: none -> 6.46 us  [shards(): with_layout_constraint((2.0 * coulomb_part).astype(jnp.bfloat16), Layout(...]
  transfers between devices with their start and end apart: 4 -> 4, of which waited for: 3 -> 3; matrix products, arithmetic and copies ran while one was open for 29% -> 16% of each run, Pallas kernels for 0% -> 0%
where the time goes in v6:
time: 381 us; the launch traced here: 377 us
  waiting for transfers between devices  182 us (48%)
  blocking collectives  76.2 us (20%)
  local copies, waits for them, and re-layouts  48.3 us (13%)
  matrix products  25.5 us (7%)
  other arithmetic  19.7 us (5%)
  between operations  14.1 us (4%)
  starting transfers between devices  10.3 us (3%)
    all_gather x1, waiting for transfers between devices, shards(): lax.all_gather(half_padded, 'dev', axis=0, tiled=True)  74.9 us
    all_gather x1, waiting for transfers between devices, shards(): lax.all_gather(orbitals, 'dev', axis=0, tiled=True)  60.4 us
    psum x1, blocking collectives, shards(): group_density = lax.psum(aux_density, 'dev')  52.2 us
    all_to_all x1, waiting for transfers between devices, shards(): lax.all_to_all(exchange_part.astype(jnp.bfloat16).reshape(row_count, grou...  46.4 us
    unnamed x1, blocking collectives  23.9 us
    unnamed x12, local copies, waits for them, and re-layouts  23.4 us
    dot_general x1, matrix products, shards(): lax.dot_general(half_flat, lax.all_gather(half_padded, 'dev', axis=0, til...  13.2 us
    dot_general x1, matrix products, shards(): jnp.dot(slab_flat, lax.all_gather(orbitals, 'dev', axis=0, tiled=True), p...  12.2 us
  transfers between devices with their start and end apart: 4, of which 3 were waited for; matrix products, arithmetic and copies ran while one was open for 16% of the time, Pallas kernels for 0%

profile of v6, /device:TPU:2, one launch (start us, length us, event | category | flops | bytes accessed | tf_op | source)
XLA Modules:
  0.0 376.6 jit_solution(13852085710437773367)
XLA Ops:
  6.5 0.0 copy-start
  6.5 0.0 all-gather.6.cloned.1.call-start
  6.5 0.7 all-gather.6.cloned.1.call-update
  7.3 0.0 all-gather.4.cloned.1.call-start
  7.3 1.1 mul.37
  8.4 0.1 mul.38
  8.5 7.3 %copy.28 = bf16[2,250,8000]{2,1,0:T(8,128)(2,1)} copy(bf16[2,250,8000]{2,0,1:T(2,128)(2,1)} %param.4) | data formatting | bytes 16000000 | tf_op args[0]
  15.8 10.0 %reshape.34 = bf16[500,8000]{1,0:T(8,128)(2,1)} reshape(bf16[2,250,8000]{2,1,0:T(8,128)(2,1)} %copy.28) | data formatting | bytes 16000000 | tf_op jit(solution)/shard_map/reshape | solution.py:15
  25.9 60.4 %all-gather.6.cloned.1.call-done = bf16[32,250,640]{2,1,0:T(8,128)(2,1)} async-done(((bf16[1,250,640]{2,1,0:T(8,128)(2,1)}), bf16[32,250,640]{2,1,0:T(8,128)(2,1)}) %all-gather.6.cloned.1.call-update) | async-done | bytes 10240016 | tf_op jit(solution)/shard_map/all_gather | solution.py:18
  86.3 10.9 %reshape.45 = bf16[8000,640]{1,0:T(8,128)(2,1)} reshape(bf16[32,250,640]{2,1,0:T(8,128)(2,1)} %all-gather.6.cloned.1.call-done) | data formatting | bytes 20480000
  97.2 0.0 copy-start.2
  97.2 12.2 %multiply_reduce_fusion = (f32[500]{0:T(512)S(1)}, bf16[500,640]{1,0:T(8,128)(2,1)S(1)}) fusion(f32[500,640]{1,0:T(8,128)S(1)} %mul.38, bf16[500,8000]{1,0:T(8,128)(2,1)} %reshape.34, bf16[8000,640]{1,0:T(8,128)(2,1)} %reshape.45), kind=kOutput, calls=%fused_computation.6 | convolution fusion | flops 5121279488 | bytes 20162000 | tf_op jit(solution)/shard_map/dot_general | solution.py:16
  109.4 0.1 reshape.36
  109.6 0.3 copy.32
  109.8 1.0 pad.4
  110.8 0.0 all-gather.4.cloned.1.call-update
  110.8 0.0 copy-done.2
  110.8 0.6 dynamic-slice.1
  111.4 0.1 reduce_sum.35
  111.5 0.1 reduce_sum.36
  112.2 52.2 %psum.7 = f32[2]{0:T(128)S(1)} all-reduce(f32[2]{0:T(128)S(1)} %reduce_sum.36), channel_id=1, replica_groups=mesh['grp'=8,'dev'=32] {'dev'}, use_global_device_ids=true, to_apply=%region_2.3 | all-reduce | flops 2 | bytes 16 | tf_op jit(solution)/shard_map/psum | solution.py:26
  164.4 0.2 dynamic-update-slice
  164.7 23.9 %all-reduce.1 = f32[16]{0:T(128)S(1)} all-reduce(f32[16]{0:T(128)S(1)} %dynamic-update-slice), channel_id=1, replica_groups=mesh['grp'=8,'dev'=32] {'grp'}, use_global_device_ids=true, to_apply=%add.1 | all-reduce | flops 16 | bytes 128
  188.6 0.0 copy-done
  188.6 0.1 convolution_bitcast_fusion
  188.7 0.1 dynamic_slice.3
  188.8 0.7 fusion.2
  189.5 7.2 %fusion = bf16[250,8000]{1,0:T(8,128)(2,1)} fusion(bf16[2,250,8000]{2,1,0:T(8,128)(2,1)} %copy.28, f32[]{:T(128)} %bitcast.5, f32[]{:T(128)} %bitcast.4), kind=kLoop, calls=%fused_computation.4 | loop fusion | flops 14000000 | bytes 12000008 | tf_op jit(solution)/shard_map/mul | solution.py:37
  196.7 6.5 %copy.31 = bf16[250,8000]{0,1:T(8,128)(2,1)} copy(bf16[250,8000]{1,0:T(8,128)(2,1)} %fusion) | data formatting | bytes 8000000 | tf_op jit(solution)/shard_map/layout_constraint | solution.py:37
  203.2 4.7 %all-to-all-start = ((bf16[250,8,1000]{0,2,1:T(8,128)(2,1)}), bf16[250,8,1000]{0,2,1:T(8,128)(2,1)}, u32[]{:S(2)}, u32[]{:S(2)}) async-start(bf16[250,8,1000]{0,2,1:T(8,128)(2,1)} %bitcast.28), calls=%async_computation | async-start | bytes 8192000 | tf_op jit(solution)/shard_map/all_to_all | solution.py:38
  207.9 74.9 %all-gather.4.cloned.1.call-done = bf16[8192,1280]{0,1:T(8,128)(2,1)} async-done(((bf16[256,1280]{0,1:T(8,128)(2,1)}), bf16[8192,1280]{0,1:T(8,128)(2,1)}) %all-gather.4.cloned.1.call-update) | async-done | bytes 20971536 | tf_op jit(solution)/shard_map/all_gather | solution.py:45
  282.8 13.2 %convolution_convert_fusion = bf16[250,8192]{1,0:T(8,128)(2,1)S(1)} fusion(bf16[250,1280]{0,1:T(8,128)(2,1)S(1)} %bitcast.30, bf16[8192,1280]{0,1:T(8,128)(2,1)} %all-gather.4.cloned.1.call-done), kind=kOutput, calls=%fused_computation | convolution fusion | flops 5244928000 | bytes 25707520 | tf_op jit(solution)/shard_map/dot_general | solution.py:43
  296.0 4.3 %copy.37 = bf16[32,8,8,1024]{3,2,1,0:T(8,128)(2,1)S(1)} copy(bf16[32,8,8,1024]{3,1,2,0:T(8,128)(2,1)S(1)} %bitcast.26) | data formatting | bytes 8388608
  300.3 0.4 slice.23
  300.7 4.2 %copy.33 = bf16[250,8,1024]{2,0,1:T(8,128)(2,1)} copy(bf16[250,8,1024]{2,1,0:T(8,128)(2,1)S(1)} %slice.23) | data formatting | bytes 8192000 | tf_op jit(solution)/shard_map/reshape | solution.py:50
  304.9 0.0 all-to-all-done
  304.9 5.6 %all-to-all-start.1 = ((bf16[250,8,1024]{2,0,1:T(8,128)(2,1)}), bf16[250,8,1024]{2,0,1:T(8,128)(2,1)}, u32[]{:S(2)}, u32[]{:S(2)}) async-start(bf16[250,8,1024]{2,0,1:T(8,128)(2,1)} %copy.33), calls=%async_computation.1 | async-start | bytes 8388608 | tf_op jit(solution)/shard_map/all_to_all | solution.py:49
  310.5 0.0 copy-start.1
  310.5 3.0 convert_reduce_fusion.1
  313.5 46.4 %all-to-all-done.1 = bf16[250,8,1024]{2,0,1:T(8,128)(2,1)} async-done(((bf16[250,8,1024]{2,0,1:T(8,128)(2,1)}), bf16[250,8,1024]{2,0,1:T(8,128)(2,1)}, u32[]{:S(2)}, u32[]{:S(2)}) %all-to-all-start.1) | async-done | bytes 4096032 | tf_op jit(solution)/shard_map/all_to_all | solution.py:49
  359.9 6.9 %convert_reduce_fusion = f32[250,1024]{1,0:T(8,128)S(1)} fusion(bf16[250,8,1024]{2,0,1:T(8,128)(2,1)} %all-to-all-done.1), kind=kLoop, calls=%fused_computation.2 | loop fusion | flops 3840000 | bytes 5120000 | tf_op jit(solution)/shard_map/reduce_sum | solution.py:53
  366.8 0.3 copy.36
  367.1 0.1 reshape.40
  367.3 2.4 subtract_add_fusion
  369.7 0.0 copy-done.1
  (1 shorter events, 0.0 us)
Async XLA Ops:
  6.5 182.1 %copy-start = (f32[16,16]{1,0:T(8,128)S(1)}, f32[16,16]{1,0:T(8,128)}, u32[]{:S(2)}) copy-start(f32[16,16]{1,0:T(8,128)} %param.7) | copy-start | bytes 3076
  6.5 79.7 %all-gather.6.cloned.1.call-start = ((), (), s32[]{:S(2)}) async-start(), calls=%async_computation.3 | async-start | bytes 10813440 | tf_op jit(solution)/shard_map/all_gather | solution.py:18
  7.3 275.5 %all-gather.4.cloned.1.call-start = ((), (), s32[]{:S(2)}) async-start(), calls=%async_computation.2 | async-start | bytes 21626880 | tf_op jit(solution)/shard_map/all_gather | solution.py:45
  97.2 13.6 %copy-start.2 = (u32[256]{0:T(256)S(1)}, u32[256]{0:T(256)}, u32[]{:S(2)}) copy-start(u32[256]{0:T(256)} %constant.25) | copy-start | bytes 3076
  203.2 101.7 %all-to-all-start = ((bf16[250,8,1000]{0,2,1:T(8,128)(2,1)}), bf16[250,8,1000]{0,2,1:T(8,128)(2,1)}, u32[]{:S(2)}, u32[]{:S(2)}) async-start(bf16[250,8,1000]{0,2,1:T(8,128)(2,1)} %bitcast.28), calls=%async_computation | async-start | bytes 8192000 | tf_op jit(solution)/shard_map/all_to_all | solution.py:38
  304.9 55.0 %all-to-all-start.1 = ((bf16[250,8,1024]{2,0,1:T(8,128)(2,1)}), bf16[250,8,1024]{2,0,1:T(8,128)(2,1)}, u32[]{:S(2)}, u32[]{:S(2)}) async-start(bf16[250,8,1024]{2,0,1:T(8,128)(2,1)} %copy.33), calls=%async_computation.1 | async-start | bytes 8388608 | tf_op jit(solution)/shard_map/all_to_all | solution.py:49
  310.5 59.2 %copy-start.1 = (f32[16,16]{1,0:T(8,128)S(1)}, f32[16,16]{1,0:T(8,128)}, u32[]{:S(2)}) copy-start(f32[16,16]{1,0:T(8,128)} %param.7) | copy-start | bytes 3076
Sparse Core Ops, SparseCore 0:
  9.2 77.0 all-gather.5
  110.9 171.8 all-gather.3
